TPU v7x, 512 devices: a whole 4x8x8 slice. The times are simulated.
512 devices in a mesh: seq: 32 (over x_lo, z, core), tensor: 16 (over x_hi, y).
Axes of the slice: x: 4 (x_hi: 2, x_lo: 2; x = x_hi * 2 + x_lo), y: 8, z: 8, core: 2. Of those that a mesh axis runs over, the one named last changes fastest.
Arguments:
- qkv: bfloat16 [3, 8192, 8192], P(None, 'seq', 'tensor'), may hold values from -6 to 6
- conv_weight: float32 [3, 3, 8192], P(None, None, 'tensor'), may hold values from -3.6 to 3.6
- decay_rate: float32 [16, 8192], P(None, 'tensor'), may hold values from 1e-05 to 0.06
- residue: float32 [16, 8192], P(None, 'tensor'), may hold values from -3 to 3
- skip_gain: float32 [8192], P('tensor'), may hold values from -5 to 5
- out_weight: bfloat16 [8192, 8192], P('seq', 'tensor'), may hold values from -0.125 to 0.125
Outputs:
- mixer_out: bfloat16 [8192, 8192], P('seq', 'tensor')
All inputs are finite; a program needn't handle non-finite values.
Results may differ from a plain program's by a relative error of at most 0.0049.
Values may be sent and summed in bfloat16 or wider, within the bound.
No kernel may reach another device: no remote copies, remote signals or barrier semaphores. Data moves between devices by JAX's collectives and lax.ppermute only.
A program may use at most 64 MiB of HBM per device.

v0:
```python
from functools import partial

import jax
import jax.numpy as jnp
from jax import lax
from jax.sharding import PartitionSpec as P

KS = 3


PRECISE = lax.Precision.HIGHEST


def passed_along(block, axis, distance):
    devices = range(lax.axis_size(axis))
    route = [(i - distance, i) for i in devices if i - distance in devices]
    return lax.ppermute(block, axis, route)


def prefix_2(part, axis, combine, identity):
    place = lax.axis_index(axis)
    gathered = jax.tree.map(lambda a: lax.all_gather(a, axis), part)
    state = jax.tree.map(lambda a, e: jnp.zeros_like(a) + jnp.asarray(e, a.dtype), part, identity)

    def one(step, state):
        return combine(
            state, jax.tree.map(lambda a: lax.dynamic_index_in_dim(a, step, 0, False), gathered)
        )

    return lax.fori_loop(0, place, one, state)


def mode_tables(rate_block, residue_block, length):
    lag_values = jnp.arange(length, dtype=jnp.float32)
    decay_table = jnp.exp(-rate_block[:, None, :] * lag_values[None, :, None])
    mode_weight = residue_block * jnp.sqrt(-jnp.expm1(-2.0 * rate_block))
    return (decay_table, mode_weight)


def toeplitz(filter_taps):
    length = filter_taps.shape[0]
    lag_index = jnp.arange(length)[:, None] - jnp.arange(length)[None, :]
    picked = filter_taps[jnp.maximum(lag_index, 0), :]
    return jnp.where(lag_index[:, :, None] >= 0, picked, 0.0)


def inner_block(block_len, inputs):
    x_block, rate_block, residue_block = inputs
    decay_table, mode_weight = mode_tables(rate_block, residue_block, block_len)
    filter_taps = jnp.einsum("mc,mdc->dc", mode_weight, decay_table, precision=PRECISE)
    inner_part = jnp.einsum("tsc,nsc->ntc", toeplitz(filter_taps), x_block, precision=PRECISE)
    local_state = jnp.einsum("msc,nsc->nmc", decay_table[:, ::-1, :], x_block, precision=PRECISE)
    block_decay = jnp.exp(-rate_block * block_len)

    def advance(state, segment):
        return (state * block_decay + segment, state)

    section_state, entering = lax.scan(
        advance, jnp.zeros(rate_block.shape, jnp.float32), local_state
    )
    return (inner_part, entering, section_state)


def carry_block(block_len, inputs):
    rate_block, residue_block, block_entering, section_entering = inputs
    decay_table, mode_weight = mode_tables(rate_block, residue_block, block_len)
    block_ids = jnp.arange(block_entering.shape[0], dtype=jnp.float32)
    reach_back = jnp.exp(-rate_block[None] * (block_len * block_ids)[:, None, None])
    entering_all = block_entering + reach_back * section_entering[None]
    later_table = decay_table * jnp.exp(-rate_block)[:, None, :]
    return jnp.einsum("mc,mdc,nmc->ndc", mode_weight, later_table, entering_all, precision=PRECISE)


def combine_modes(earlier, later):
    return (earlier[0] * later[0], earlier[1] * later[0] + later[1])


def local(qkv, conv_weight, decay_rate, residue, skip_gain, out_weight):
    tokens_here = qkv.shape[1]
    channels = qkv.shape[2]
    modes = decay_rate.shape[0]
    tail_rows = qkv[:, tokens_here - (KS - 1) :, :]
    previous = passed_along(tail_rows, "seq", 1)
    extended = jnp.concatenate([previous, qkv], axis=1).astype(jnp.float32)
    filtered = jnp.zeros((3, tokens_here, channels), jnp.float32)
    for offset in range(KS):
        start_row = KS - 1 - offset
        filtered = (
            filtered
            + conv_weight[:, offset, None, :] * extended[:, start_row : start_row + tokens_here, :]
        )
    product = filtered[1] * filtered[2]
    group_width = min(channels, 128)
    groups = channels // group_width
    block_len = min(tokens_here, 64)
    block_count = tokens_here // block_len
    x_groups = product.reshape(block_count, block_len, groups, group_width).transpose(2, 0, 1, 3)
    rate_groups = decay_rate.reshape(modes, groups, group_width).transpose(1, 0, 2)
    residue_groups = residue.reshape(modes, groups, group_width).transpose(1, 0, 2)
    inner_part, block_entering, section_state = lax.map(
        partial(inner_block, block_len), (x_groups, rate_groups, residue_groups)
    )
    section_state = section_state.transpose(1, 0, 2).reshape(modes, channels)
    section_decay = jnp.exp(-decay_rate * tokens_here)
    identity = (
        jnp.ones(section_state.shape, jnp.float32),
        jnp.zeros(section_state.shape, jnp.float32),
    )
    prefix = prefix_2((section_decay, section_state), "seq", combine_modes, identity)
    section_entering = prefix[1].reshape(modes, groups, group_width).transpose(1, 0, 2)
    carried = lax.map(
        partial(carry_block, block_len),
        (rate_groups, residue_groups, block_entering, section_entering),
    )
    long_part = (inner_part + carried).transpose(1, 2, 0, 3).reshape(tokens_here, channels)
    long_part = long_part + skip_gain[None, :] * product
    mixed_local = (filtered[0] * long_part).astype(jnp.bfloat16)
    features = lax.all_gather(mixed_local, "tensor", axis=1, tiled=True)
    projected = jnp.dot(
        features,
        lax.all_gather(out_weight, "seq", axis=0, tiled=True),
        preferred_element_type=jnp.float32,
    )
    return projected.astype(jnp.bfloat16)


def solution(mesh):
    return jax.shard_map(
        local,
        mesh=mesh,
        in_specs=(
            P(None, "seq", "tensor"),
            P(None, None, "tensor"),
            P(None, "tensor"),
            P(None, "tensor"),
            P("tensor"),
            P("seq", "tensor"),
        ),
        out_specs=P("seq", "tensor"),
        check_vma=False,
    )
```

profile of v0, /device:TPU:1, one launch (start us, length us, event | category | flops | bytes accessed | tf_op | source)
XLA Modules:
  0.0 445.3 jit_solution(3757608169586370454)
XLA Ops:
  7.4 5.4 %collective-permute-start = (bf16[3,2,512]{2,1,0:T(2,128)(2,1)S(1)}, bf16[3,2,512]{2,1,0:T(2,128)(2,1)S(1)}, u32[]{:S(2)}, u32[]{:S(2)}) collective-permute-start(bf16[3,2,512]{2,1,0:T(2,128)(2,1)S(1)} %slice.31), channel_id=1, source_target_pairs={{0,16},{16,32},{32,48},{48,64},{64,80},{80,96},{96,112},{112,128},... | collective-permute-start | bytes 18440 | tf_op jit(solution)/shard_map/ppermute | solution.py:17
  20.4 119.2 %while.50 = (s32[]{:T(128)}, f32[4,4,64,128]{2,1,3,0:T(4,128)}, f32[4,4,16,128]{3,2,1,0:T(8,128)}, f32[4,16,128]{2,1,0:T(8,128)}, f32[4,4,64,128]{3,0,2,1:T(4,12...) while((s32[]{:T(128)}, f32[4,4,64,128]{2,1,3,0:T(4,128)}, ...), condition=%wide.region_3.4_spmd, body=%wide.region_0.3_spmd.sunk | while | flops 32536580 | bytes 16271129 | solution.py:100
  21.7 1.8 convolution_bitcast_fusion.3
  25.9 10.8 %gather_fusion = f32[4096,128]{1,0:T(8,128)S(1)} fusion(f32[64,128]{1,0:T(8,128)S(1)} %bitcast.132, s32[4096]{0:T(1024)S(1)} %broadcast_clamp_fusion.2), kind=kCustom, calls=%fused_computation.clone.1 | custom fusion | bytes 4210688 | tf_op jit(solution)/shard_map/while/body/eval_jaxpr/gather | solution.py:43
  36.7 4.5 %copy.70 = f32[64,64,128]{1,0,2:T(8,128)} copy(f32[64,64,128]{2,1,0:T(8,128)S(1)} %bitcast.133) | data formatting | bytes 4194304 | tf_op jit(solution)/shard_map/while/body/eval_jaxpr/gather | solution.py:43
  41.2 9.0 %fusion.52 = f32[4,4,64,128]{2,1,3,0:T(4,128)} fusion(f32[4,4,64,128]{2,1,3,0:T(4,128)} %get-tuple-element.485, s32[]{:T(128)} %get-tuple-element.484, f32[64,64,128]{1,0,2:T(8,128)} %copy.70, pred[64,64]{1,0:T(8,128)(4,1)S(1)} %subtract_compare_fusion.2, f32[1,4,64,128]{2,1,3,0:T(4,128)S(1)} %copy.71), kind=kOutput, calls=%fused_computation.32.clone.1 | convolution fusion | flops 25690112 | bytes 4592128 | tf_op jit(solution)/shard_map/while/body/eval_jaxpr/tsc,nsc->ntc/dot_general | solution.py:51
  51.5 1.8 convolution_bitcast_fusion.3
  55.7 10.8 %gather_fusion = f32[4096,128]{1,0:T(8,128)S(1)} fusion(f32[64,128]{1,0:T(8,128)S(1)} %bitcast.132, s32[4096]{0:T(1024)S(1)} %broadcast_clamp_fusion.2), kind=kCustom, calls=%fused_computation.clone.1 | custom fusion | bytes 4210688 | tf_op jit(solution)/shard_map/while/body/eval_jaxpr/gather | solution.py:43
  66.5 4.5 %copy.70 = f32[64,64,128]{1,0,2:T(8,128)} copy(f32[64,64,128]{2,1,0:T(8,128)S(1)} %bitcast.133) | data formatting | bytes 4194304 | tf_op jit(solution)/shard_map/while/body/eval_jaxpr/gather | solution.py:43
  71.0 9.0 %fusion.52 = f32[4,4,64,128]{2,1,3,0:T(4,128)} fusion(f32[4,4,64,128]{2,1,3,0:T(4,128)} %get-tuple-element.485, s32[]{:T(128)} %get-tuple-element.484, f32[64,64,128]{1,0,2:T(8,128)} %copy.70, pred[64,64]{1,0:T(8,128)(4,1)S(1)} %subtract_compare_fusion.2, f32[1,4,64,128]{2,1,3,0:T(4,128)S(1)} %copy.71), kind=kOutput, calls=%fused_computation.32.clone.1 | convolution fusion | flops 25690112 | bytes 4592128 | tf_op jit(solution)/shard_map/while/body/eval_jaxpr/tsc,nsc->ntc/dot_general | solution.py:51
  81.3 1.8 convolution_bitcast_fusion.3
  85.5 10.8 %gather_fusion = f32[4096,128]{1,0:T(8,128)S(1)} fusion(f32[64,128]{1,0:T(8,128)S(1)} %bitcast.132, s32[4096]{0:T(1024)S(1)} %broadcast_clamp_fusion.2), kind=kCustom, calls=%fused_computation.clone.1 | custom fusion | bytes 4210688 | tf_op jit(solution)/shard_map/while/body/eval_jaxpr/gather | solution.py:43
  96.3 4.5 %copy.70 = f32[64,64,128]{1,0,2:T(8,128)} copy(f32[64,64,128]{2,1,0:T(8,128)S(1)} %bitcast.133) | data formatting | bytes 4194304 | tf_op jit(solution)/shard_map/while/body/eval_jaxpr/gather | solution.py:43
  100.8 9.0 %fusion.52 = f32[4,4,64,128]{2,1,3,0:T(4,128)} fusion(f32[4,4,64,128]{2,1,3,0:T(4,128)} %get-tuple-element.485, s32[]{:T(128)} %get-tuple-element.484, f32[64,64,128]{1,0,2:T(8,128)} %copy.70, pred[64,64]{1,0:T(8,128)(4,1)S(1)} %subtract_compare_fusion.2, f32[1,4,64,128]{2,1,3,0:T(4,128)S(1)} %copy.71), kind=kOutput, calls=%fused_computation.32.clone.1 | convolution fusion | flops 25690112 | bytes 4592128 | tf_op jit(solution)/shard_map/while/body/eval_jaxpr/tsc,nsc->ntc/dot_general | solution.py:51
  111.1 1.8 convolution_bitcast_fusion.3
  115.3 10.8 %gather_fusion = f32[4096,128]{1,0:T(8,128)S(1)} fusion(f32[64,128]{1,0:T(8,128)S(1)} %bitcast.132, s32[4096]{0:T(1024)S(1)} %broadcast_clamp_fusion.2), kind=kCustom, calls=%fused_computation.clone.1 | custom fusion | bytes 4210688 | tf_op jit(solution)/shard_map/while/body/eval_jaxpr/gather | solution.py:43
  126.1 4.5 %copy.70 = f32[64,64,128]{1,0,2:T(8,128)} copy(f32[64,64,128]{2,1,0:T(8,128)S(1)} %bitcast.133) | data formatting | bytes 4194304 | tf_op jit(solution)/shard_map/while/body/eval_jaxpr/gather | solution.py:43
  130.6 9.0 %fusion.52 = f32[4,4,64,128]{2,1,3,0:T(4,128)} fusion(f32[4,4,64,128]{2,1,3,0:T(4,128)} %get-tuple-element.485, s32[]{:T(128)} %get-tuple-element.484, f32[64,64,128]{1,0,2:T(8,128)} %copy.70, pred[64,64]{1,0:T(8,128)(4,1)S(1)} %subtract_compare_fusion.2, f32[1,4,64,128]{2,1,3,0:T(4,128)S(1)} %copy.71), kind=kOutput, calls=%fused_computation.32.clone.1 | convolution fusion | flops 25690112 | bytes 4592128 | tf_op jit(solution)/shard_map/while/body/eval_jaxpr/tsc,nsc->ntc/dot_general | solution.py:51
  141.1 70.4 %all-gather.6.cloned.1.call-done = f32[32,16,512]{2,1,0:T(8,128)} async-done(((f32[1,16,512]{2,1,0:T(8,128)}), f32[32,16,512]{2,1,0:T(8,128)}) %all-gather.6.cloned.1.call-update) | async-done | bytes 1048592 | tf_op jit(solution)/shard_map/all_gather | solution.py:22
  212.6 11.1 %while.52 = (s32[]{:T(128)}, f32[4,4,64,128]{2,1,3,0:T(4,128)S(1)}, f32[4,4,16,128]{3,2,1,0:T(8,128)}, f32[4,16,128]{1,2,0:T(8,128)S(1)}, f32[4,16,128]{1,2,0:T(...) while((s32[]{:T(128)}, f32[4,4,64,128]{2,1,3,0:T(4,128)S(1)}, f32[4,4,16,128]{3,2,1,0:T(8,128)}, ...), condition=%wide.region_7.8_spmd, body=%wide.region_6.7_spmd.sunk | while | flops 6594566 | bytes 1049197 | solution.py:111
  213.7 1.7 fusion.56
  226.9 126.3 %all-gather.8.cloned.1.call-done = bf16[256,8192]{1,0:T(8,128)(2,1)} async-done(((bf16[256,512]{1,0:T(8,128)(2,1)}), bf16[256,8192]{1,0:T(8,128)(2,1)}) %all-gather.8.cloned.1.call-update) | async-done | bytes 4194320 | tf_op jit(solution)/shard_map/all_gather | solution.py:118
  353.2 77.9 %all-gather.10.cloned.1.call-done = bf16[8192,512]{1,0:T(8,128)(2,1)} async-done(((bf16[256,512]{1,0:T(8,128)(2,1)}), bf16[8192,512]{1,0:T(8,128)(2,1)}) %all-gather.10.cloned.1.call-update) | async-done | bytes 8388624 | tf_op jit(solution)/shard_map/all_gather | solution.py:121
  431.1 7.7 %convolution_convert_fusion = bf16[256,512]{1,0:T(8,128)(2,1)} fusion(bf16[256,8192]{1,0:T(8,128)(2,1)} %all-gather.8.cloned.1.call-done, bf16[8192,512]{1,0:T(8,128)(2,1)} %all-gather.10.cloned.1.call-done), kind=kOutput, calls=%fused_computation.53 | convolution fusion | flops 2147614720 | bytes 12845056 | tf_op jit(solution)/shard_map/dot_general | solution.py:119
  (182 shorter events, 39.1 us)
Async XLA Ops:
  6.5 10.6 %copy-start.3 = (bf16[3,256,512]{2,1,0:T(8,128)(2,1)S(1)}, bf16[3,256,512]{2,1,0:T(8,128)(2,1)}, u32[]{:S(2)}) copy-start(bf16[3,256,512]{2,1,0:T(8,128)(2,1)} %param.14) | copy-start | bytes 2359300
  6.5 134.6 %all-gather.12.cloned.1.call-start = ((), (), s32[]{:S(2)}) async-start(), calls=%async_computation.3 | async-start | bytes 1081344 | tf_op jit(solution)/shard_map/all_gather | solution.py:22
  7.4 9.8 %collective-permute-start = (bf16[3,2,512]{2,1,0:T(2,128)(2,1)S(1)}, bf16[3,2,512]{2,1,0:T(2,128)(2,1)S(1)}, u32[]{:S(2)}, u32[]{:S(2)}) collective-permute-start(bf16[3,2,512]{2,1,0:T(2,128)(2,1)S(1)} %slice.31), channel_id=1, source_target_pairs={{0,16},{16,32},{32,48},{48,64},{64,80},{80,96},{96,112},{112,128},... | collective-permute-start | bytes 18440 | tf_op jit(solution)/shard_map/ppermute | solution.py:17
  14.2 197.3 %all-gather.6.cloned.1.call-start = ((), (), s32[]{:S(2)}) async-start(), calls=%async_computation | async-start | bytes 1081344 | tf_op jit(solution)/shard_map/all_gather | solution.py:22
  17.8 1.2 copy-start
  141.0 212.1 %all-gather.8.cloned.1.call-start = ((), (), s32[]{:S(2)}) async-start(), calls=%async_computation.1 | async-start | bytes 4456448 | tf_op jit(solution)/shard_map/all_gather | solution.py:118
  212.6 11.1 %copy-start.2 = (f32[4,4,64,128]{2,1,3,0:T(4,128)S(1)}, f32[4,4,64,128]{2,1,3,0:T(4,128)}, u32[]{:S(2)}) copy-start(f32[4,4,64,128]{2,1,3,0:T(4,128)} %get-tuple-element.148) | copy-start | bytes 1572868
  224.0 1.4 copy-start.1
  224.0 1.4 copy-start.4
  226.3 204.8 %all-gather.10.cloned.1.call-start = ((), (), s32[]{:S(2)}) async-start(), calls=%async_computation.2 | async-start | bytes 8650752 | tf_op jit(solution)/shard_map/all_gather | solution.py:121
Sparse Core Ops, SparseCore 0:
  14.3 70.3 all-gather.11
  141.2 70.2 all-gather.5
  226.5 126.6 all-gather.7
  355.2 75.8 all-gather.9
where the time goes:
time: 448 us; the launch traced here: 445 us
  waiting for transfers between devices  275 us (61%)
  local copies, waits for them, and re-layouts  83.7 us (19%)
  matrix products  57.6 us (13%)
  between operations  13.3 us (3%)
  other arithmetic  9.04 us (2%)
  starting transfers between devices  5.51 us (1%)
    all_gather x1, waiting for transfers between devices, local(): features = lax.all_gather(mixed_local, 'tensor', axis=1, tiled=True)  126 us
    all_gather x1, waiting for transfers between devices, local(): lax.all_gather(out_weight, 'seq', axis=0, tiled=True)  77.9 us
    all_gather x2, waiting for transfers between devices, prefix_2(): gathered = jax.tree.map(lambda a: lax.all_gather(a, axis), part)  70.4 us
    gather x8, local copies, waits for them, and re-layouts, toeplitz(): picked = filter_taps[jnp.maximum(lag_index, 0), :]  61.1 us
    dot_general x4, matrix products, inner_block(): jnp.einsum('tsc,nsc->ntc', toeplitz(filter_taps), x_block, precision=PREC...  36 us
  transfers between devices with their start and end apart: 5, of which 3 were waited for; matrix products, arithmetic and copies ran while one was open for 28% of the time, Pallas kernels for 0%

commit v1 on v0

v1 whole, which is shorter than its diff:
```python
import jax
import jax.numpy as jnp
from jax import lax
from jax.sharding import PartitionSpec as P


KS = 3


PRECISE = lax.Precision.HIGHEST


def passed_along(block, axis, distance):
    devices = range(lax.axis_size(axis))
    route = [(i - distance, i) for i in devices if i - distance in devices]
    return lax.ppermute(block, axis, route)


def entering_state(local_state, rate, tokens_here, axis):
    sections = lax.axis_size(axis)
    decay = jnp.exp(-rate * tokens_here)
    state = passed_along(local_state, axis, 1)
    if sections > 2:
        state = state + decay * passed_along(local_state, axis, 2)
    distance = 2
    while distance < sections:
        state = state + jnp.exp(-rate * (tokens_here * distance)) * passed_along(state, axis, distance)
        distance *= 2
    return state


def body(qkv, conv_weight, decay_rate, residue, skip_gain, out_weight):
    tokens_here = qkv.shape[1]
    channels = qkv.shape[2]
    tail_rows = qkv[:, tokens_here - (KS - 1) :, :]
    previous = passed_along(tail_rows, "seq", 1)
    extended = jnp.concatenate([previous, qkv], axis=1).astype(jnp.float32)
    filtered = jnp.zeros((3, tokens_here, channels), jnp.float32)
    for offset in range(KS):
        start_row = KS - 1 - offset
        filtered = (
            filtered
            + conv_weight[:, offset, None, :] * extended[:, start_row : start_row + tokens_here, :]
        )
    product = filtered[1] * filtered[2]

    return finish(filtered, product, decay_rate, residue, skip_gain, out_weight)


def finish(filtered, product, decay_rate, residue, skip_gain, out_weight):
    tokens_here, channels = product.shape
    modes = decay_rate.shape[0]
    rate = decay_rate
    mode_weight = residue * jnp.sqrt(-jnp.expm1(-2.0 * rate))
    lags = jnp.arange(tokens_here, dtype=jnp.float32)[:, None, None]
    growth = jnp.exp(rate[None] * lags)
    scaled = (growth * product[:, None, :]).reshape(tokens_here, modes * channels)
    lower = (jnp.arange(tokens_here)[:, None] >= jnp.arange(tokens_here)[None, :]).astype(jnp.float32)
    running = jnp.dot(lower, scaled, precision=PRECISE).reshape(tokens_here, modes, channels)
    local_state = jnp.exp(-rate * (tokens_here - 1)) * running[tokens_here - 1]
    section_entering = entering_state(local_state, rate, tokens_here, "seq")
    shrink = jnp.exp(-rate[None] * lags)
    total = running + jnp.exp(-rate) * section_entering
    long_part = jnp.sum(mode_weight[None] * shrink * total, axis=1)
    long_part = long_part + skip_gain[None, :] * product
    mixed_local = (filtered[0] * long_part).astype(jnp.bfloat16)
    features = lax.all_gather(mixed_local, "tensor", axis=1, tiled=True)
    weight_all = lax.all_gather(out_weight, "seq", axis=0, tiled=True)
    projected = jnp.dot(
        features,
        weight_all,
        preferred_element_type=jnp.float32,
    )
    return projected.astype(jnp.bfloat16)


def solution(mesh):
    return jax.shard_map(
        body,
        mesh=mesh,
        in_specs=(
            P(None, "seq", "tensor"),
            P(None, None, "tensor"),
            P(None, "tensor"),
            P(None, "tensor"),
            P("tensor"),
            P("seq", "tensor"),
        ),
        out_specs=P("seq", "tensor"),
        check_vma=False,
    )
```

time: 448 us -> 293 us (0.65)
  waiting for transfers between devices: 275 us -> 191 us
  local copies, waits for them, and re-layouts: 83.7 us -> 25.8 us
  matrix products: 57.6 us -> 13.8 us
  starting transfers between devices: 5.51 us -> 41.6 us
    all_gather x4 -> x2, waiting for transfers between devices: 275 us -> 184 us  [the longest x1 106 us: finish(): features = lax.all_gather(mixed_local, 'tensor', axis=1, tiled=True)]
    gather x8 -> x0, local copies, waits for them, and re-layouts: 61.1 us -> none  [toeplitz(): picked = filter_taps[jnp.maximum(lag_index, 0), :]]
    dot_general x13 -> x2, matrix products: 57.6 us -> 13.8 us  [the longest x1 7.69 us: finish(): jnp.dot(features, weight_all, preferred_element_type=jnp.float32)]
    ppermute x1 -> x7, starting transfers between devices: 5.38 us -> 41.6 us  [passed_along(): return lax.ppermute(block, axis, route)]
    unnamed x14 -> x13, local copies, waits for them, and re-layouts: 3.53 us -> 23 us
    ppermute x1 -> x7, waiting for transfers between devices: 0.01 us -> 5.73 us  [passed_along(): return lax.ppermute(block, axis, route)]
    dynamic_update_slice x8 -> x0, local copies, waits for them, and re-layouts: 4.88 us -> none  [local(): lax.map(partial(inner_block, block_len), (x_groups, rate_groups, residue_...]
    dynamic_slice x16 -> x0, local copies, waits for them, and re-layouts: 4.87 us -> none  [the longest x8 3.72 us: local(): lax.map(partial(carry_block, block_len), (rate_groups, residue_groups, bl...]
  transfers between devices with their start and end apart: 5 -> 9, of which waited for: 3 -> 7; matrix products, arithmetic and copies ran while one was open for 28% -> 4% of each run, Pallas kernels for 0% -> 0%
where the time goes in v1:
time: 293 us; the launch traced here: 292 us
  waiting for transfers between devices  191 us (65%)
  starting transfers between devices  41.6 us (14%)
  local copies, waits for them, and re-layouts  25.8 us (9%)
  matrix products  13.8 us (5%)
  between operations  13.6 us (5%)
  other arithmetic  6.91 us (2%)
    all_gather x1, waiting for transfers between devices, finish(): features = lax.all_gather(mixed_local, 'tensor', axis=1, tiled=True)  106 us
    all_gather x1, waiting for transfers between devices, finish(): weight_all = lax.all_gather(out_weight, 'seq', axis=0, tiled=True)  78.1 us
    ppermute x7, starting transfers between devices, passed_along(): return lax.ppermute(block, axis, route)  41.6 us
    unnamed x13, local copies, waits for them, and re-layouts  23 us
    dot_general x1, matrix products, finish(): jnp.dot(features, weight_all, preferred_element_type=jnp.float32)  7.69 us
    dot_general x1, matrix products, finish(): jnp.dot(lower, scaled, precision=PRECISE)  6.09 us
  transfers between devices with their start and end apart: 9, of which 7 were waited for; matrix products, arithmetic and copies ran while one was open for 4% of the time, Pallas kernels for 0%

profile of v1, /device:TPU:1, one launch (start us, length us, event | category | flops | bytes accessed | tf_op | source)
XLA Modules:
  0.0 292.3 jit_solution(11436946536980711799)
XLA Ops:
  7.3 5.4 %collective-permute-start = (bf16[3,2,512]{2,1,0:T(2,128)(2,1)S(1)}, bf16[3,2,512]{2,1,0:T(2,128)(2,1)S(1)}, u32[]{:S(2)}, u32[]{:S(2)}) collective-permute-start(bf16[3,2,512]{2,1,0:T(2,128)(2,1)S(1)} %slice.35), channel_id=1, source_target_pairs={{0,16},{16,32},{32,48},{48,64},{64,80},{80,96},{96,112},{112,128},... | collective-permute-start | bytes 18440 | tf_op jit(solution)/shard_map/ppermute | solution.py:16
  12.7 0.9 fusion.13
  14.3 1.7 collective-permute-done
  16.1 1.4 maximum_convert_fusion
  18.0 1.1 mul.191
  19.1 8.0 %copy.11 = f32[32,8,16,512]{3,1,2,0:T(8,128)S(1)} copy(f32[32,8,16,512]{3,2,1,0:T(8,128)S(1)} %bitcast.32) | data formatting | bytes 16777216
  27.1 6.1 %fusion.2 = f32[256,8192]{1,0:T(8,128)S(1)} fusion(f32[256,8192]{1,0:T(8,128)S(1)} %bitcast.31, f32[8192]{0:T(1024)S(1)} %bitcast.34), kind=kOutput, calls=%fused_computation.3 | convolution fusion | flops 6446710784 | bytes 16809984 | tf_op jit(solution)/shard_map/dot_general | solution.py:59
  33.2 3.2 %copy-done = f32[256,8192]{1,0:T(8,128)} copy-done((f32[256,8192]{1,0:T(8,128)}, f32[256,8192]{1,0:T(8,128)S(1)}, u32[]{:S(2)}) %copy-start) | copy-done | bytes 8388632
  36.6 1.9 collective-permute-start.1
  38.5 3.6 %collective-permute-start.2 = (f32[16,512]{1,0:T(8,128)S(1)}, f32[16,512]{1,0:T(8,128)S(1)}, u32[]{:S(2)}, u32[]{:S(2)}) collective-permute-start(f32[16,512]{1,0:T(8,128)S(1)} %exponential_multiply_fusion), channel_id=1, source_target_pairs={{0,32},{16,48},{32,64},{48,80},{64,96},{80,112},{96,128},{112,144}... | collective-permute-start | bytes 98312 | tf_op jit(solution)/shard_map/ppermute | solution.py:16
  42.1 1.0 collective-permute-done.2
  43.2 4.0 %collective-permute-start.3 = (f32[16,512]{1,0:T(8,128)S(1)}, f32[16,512]{1,0:T(8,128)S(1)}, u32[]{:S(2)}, u32[]{:S(2)}) collective-permute-start(f32[16,512]{1,0:T(8,128)S(1)} %multiply_add_fusion.3), channel_id=1, source_target_pairs={{0,32},{16,48},{32,64},{48,80},{64,96},{80,112},{96,128},{112,144}... | collective-permute-start | bytes 98312 | tf_op jit(solution)/shard_map/ppermute | solution.py:16
  47.2 1.0 collective-permute-done.3
  48.2 7.9 %collective-permute-start.4 = (f32[16,512]{1,0:T(8,128)S(1)}, f32[16,512]{1,0:T(8,128)S(1)}, u32[]{:S(2)}, u32[]{:S(2)}) collective-permute-start(f32[16,512]{1,0:T(8,128)S(1)} %multiply_add_fusion.2), channel_id=1, source_target_pairs={{0,64},{16,80},{32,96},{48,112},{64,128},{80,144},{96,160},{112,17... | collective-permute-start | bytes 98312 | tf_op jit(solution)/shard_map/ppermute | solution.py:16
  56.1 1.0 collective-permute-done.4
  57.1 9.4 %collective-permute-start.5 = (f32[16,512]{1,0:T(8,128)S(1)}, f32[16,512]{1,0:T(8,128)S(1)}, u32[]{:S(2)}, u32[]{:S(2)}) collective-permute-start(f32[16,512]{1,0:T(8,128)S(1)} %multiply_add_fusion.1), channel_id=1, source_target_pairs={{0,128},{16,144},{32,160},{48,176},{64,192},{80,208},{96,224},{112... | collective-permute-start | bytes 98312 | tf_op jit(solution)/shard_map/ppermute | solution.py:16
  66.5 1.0 collective-permute-done.5
  67.5 9.4 %collective-permute-start.6 = (f32[16,512]{1,0:T(8,128)S(1)}, f32[16,512]{1,0:T(8,128)S(1)}, u32[]{:S(2)}, u32[]{:S(2)}) collective-permute-start(f32[16,512]{1,0:T(8,128)S(1)} %multiply_add_fusion), channel_id=1, source_target_pairs={{0,256},{16,272},{32,288},{48,304},{64,320},{80,336},{96,352},{112... | collective-permute-start | bytes 98312 | tf_op jit(solution)/shard_map/ppermute | solution.py:16
  76.9 11.0 %copy.12 = f32[32,8,16,512]{3,2,1,0:T(8,128)S(1)} copy(f32[32,8,16,512]{3,1,2,0:T(8,128)} %bitcast.30) | data formatting | bytes 16777216
  87.9 3.9 %fusion.1 = f32[256,512]{1,0:T(8,128)S(1)} fusion(f32[32,8,16,512]{3,2,1,0:T(8,128)S(1)} %copy.12, f32[16,512]{1,0:T(8,128)S(1)} %get-tuple-element.6, f32[16,512]{1,0:T(8,128)S(1)} %get-tuple-element.7, f32[16,512]{1,0:T(8,128)S(1)} %get-tuple-element.5), kind=kLoop, calls=%fused_computation.2 | loop fusion | flops 10354688 | bytes 9011200 | tf_op jit(solution)/shard_map/reduce_sum | solution.py:64
  91.9 0.9 fusion.12
  93.6 106.1 %all-gather.3.cloned.1.call-done = bf16[256,8192]{1,0:T(8,128)(2,1)} async-done(((bf16[256,512]{1,0:T(8,128)(2,1)}), bf16[256,8192]{1,0:T(8,128)(2,1)}) %all-gather.3.cloned.1.call-update) | async-done | bytes 4194320 | tf_op jit(solution)/shard_map/all_gather | solution.py:67
  199.7 78.1 %all-gather.5.cloned.1.call-done = bf16[8192,512]{1,0:T(8,128)(2,1)} async-done(((bf16[256,512]{1,0:T(8,128)(2,1)}), bf16[8192,512]{1,0:T(8,128)(2,1)}) %all-gather.5.cloned.1.call-update) | async-done | bytes 8388624 | tf_op jit(solution)/shard_map/all_gather | solution.py:68
  277.8 7.7 %convolution_convert_fusion = bf16[256,512]{1,0:T(8,128)(2,1)} fusion(bf16[256,8192]{1,0:T(8,128)(2,1)} %all-gather.3.cloned.1.call-done, bf16[8192,512]{1,0:T(8,128)(2,1)} %all-gather.5.cloned.1.call-done), kind=kOutput, calls=%fused_computation.14 | convolution fusion | flops 2147614720 | bytes 12845056 | tf_op jit(solution)/shard_map/dot_general | solution.py:69
  (27 shorter events, 3.1 us)
Async XLA Ops:
  6.5 193.2 %all-gather.3.cloned.1.call-start = ((), (), s32[]{:S(2)}) async-start(), calls=%async_computation | async-start | bytes 4456448 | tf_op jit(solution)/shard_map/all_gather | solution.py:67
  7.3 8.8 %collective-permute-start = (bf16[3,2,512]{2,1,0:T(2,128)(2,1)S(1)}, bf16[3,2,512]{2,1,0:T(2,128)(2,1)S(1)}, u32[]{:S(2)}, u32[]{:S(2)}) collective-permute-start(bf16[3,2,512]{2,1,0:T(2,128)(2,1)S(1)} %slice.35), channel_id=1, source_target_pairs={{0,16},{16,32},{32,48},{48,64},{64,80},{80,96},{96,112},{112,128},... | collective-permute-start | bytes 18440 | tf_op jit(solution)/shard_map/ppermute | solution.py:16
  27.1 9.4 %copy-start.1 = (f32[16,512]{1,0:T(8,128)S(1)}, f32[16,512]{1,0:T(8,128)}, u32[]{:S(2)}) copy-start(f32[16,512]{1,0:T(8,128)} %param.8) | copy-start | bytes 98308
  33.2 3.2 %copy-start = (f32[256,8192]{1,0:T(8,128)}, f32[256,8192]{1,0:T(8,128)S(1)}, u32[]{:S(2)}) copy-start(f32[256,8192]{1,0:T(8,128)S(1)} %fusion.2) | copy-start | bytes 25165828
  36.6 5.6 %collective-permute-start.1 = (f32[16,512]{1,0:T(8,128)S(1)}, f32[16,512]{1,0:T(8,128)S(1)}, u32[]{:S(2)}, u32[]{:S(2)}) collective-permute-start(f32[16,512]{1,0:T(8,128)S(1)} %exponential_multiply_fusion), channel_id=1, source_target_pairs={{0,16},{16,32},{32,48},{48,64},{64,80},{80,96},{96,112},{112,128},... | collective-permute-start | bytes 98312 | tf_op jit(solution)/shard_map/ppermute | solution.py:16
  38.5 4.6 %collective-permute-start.2 = (f32[16,512]{1,0:T(8,128)S(1)}, f32[16,512]{1,0:T(8,128)S(1)}, u32[]{:S(2)}, u32[]{:S(2)}) collective-permute-start(f32[16,512]{1,0:T(8,128)S(1)} %exponential_multiply_fusion), channel_id=1, source_target_pairs={{0,32},{16,48},{32,64},{48,80},{64,96},{80,112},{96,128},{112,144}... | collective-permute-start | bytes 98312 | tf_op jit(solution)/shard_map/ppermute | solution.py:16
  43.2 5.0 %collective-permute-start.3 = (f32[16,512]{1,0:T(8,128)S(1)}, f32[16,512]{1,0:T(8,128)S(1)}, u32[]{:S(2)}, u32[]{:S(2)}) collective-permute-start(f32[16,512]{1,0:T(8,128)S(1)} %multiply_add_fusion.3), channel_id=1, source_target_pairs={{0,32},{16,48},{32,64},{48,80},{64,96},{80,112},{96,128},{112,144}... | collective-permute-start | bytes 98312 | tf_op jit(solution)/shard_map/ppermute | solution.py:16
  48.2 8.9 %collective-permute-start.4 = (f32[16,512]{1,0:T(8,128)S(1)}, f32[16,512]{1,0:T(8,128)S(1)}, u32[]{:S(2)}, u32[]{:S(2)}) collective-permute-start(f32[16,512]{1,0:T(8,128)S(1)} %multiply_add_fusion.2), channel_id=1, source_target_pairs={{0,64},{16,80},{32,96},{48,112},{64,128},{80,144},{96,160},{112,17... | collective-permute-start | bytes 98312 | tf_op jit(solution)/shard_map/ppermute | solution.py:16
  57.1 10.4 %collective-permute-start.5 = (f32[16,512]{1,0:T(8,128)S(1)}, f32[16,512]{1,0:T(8,128)S(1)}, u32[]{:S(2)}, u32[]{:S(2)}) collective-permute-start(f32[16,512]{1,0:T(8,128)S(1)} %multiply_add_fusion.1), channel_id=1, source_target_pairs={{0,128},{16,144},{32,160},{48,176},{64,192},{80,208},{96,224},{112... | collective-permute-start | bytes 98312 | tf_op jit(solution)/shard_map/ppermute | solution.py:16
  67.5 20.4 %collective-permute-start.6 = (f32[16,512]{1,0:T(8,128)S(1)}, f32[16,512]{1,0:T(8,128)S(1)}, u32[]{:S(2)}, u32[]{:S(2)}) collective-permute-start(f32[16,512]{1,0:T(8,128)S(1)} %multiply_add_fusion), channel_id=1, source_target_pairs={{0,256},{16,272},{32,288},{48,304},{64,320},{80,336},{96,352},{112... | collective-permute-start | bytes 98312 | tf_op jit(solution)/shard_map/ppermute | solution.py:16
  76.9 11.0 %copy-start.2 = (f32[16,512]{1,0:T(8,128)S(1)}, f32[16,512]{1,0:T(8,128)}, u32[]{:S(2)}) copy-start(f32[16,512]{1,0:T(8,128)} %param.9) | copy-start | bytes 98308
  87.9 4.0 %copy-start.3 = (f32[512]{0:T(512)S(1)}, f32[512]{0:T(512)}, u32[]{:S(2)}) copy-start(f32[512]{0:T(512)} %param.10) | copy-start | bytes 6148
  92.9 184.9 %all-gather.5.cloned.1.call-start = ((), (), s32[]{:S(2)}) async-start(), calls=%async_computation.1 | async-start | bytes 8650752 | tf_op jit(solution)/shard_map/all_gather | solution.py:68
Sparse Core Ops, SparseCore 0:
  93.0 106.7 all-gather.2
  201.9 75.8 all-gather.4

commit v2 on v1

--- a/solution.py
+++ b/solution.py
@@ -64,11 +64,15 @@
     long_part = jnp.sum(mode_weight[None] * shrink * total, axis=1)
     long_part = long_part + skip_gain[None, :] * product
     mixed_local = (filtered[0] * long_part).astype(jnp.bfloat16)
-    features = lax.all_gather(mixed_local, "tensor", axis=1, tiled=True)
+    groups = lax.axis_size("tensor")
+    spread = jnp.broadcast_to(mixed_local[None], (groups,) + mixed_local.shape)
+    features = lax.all_to_all(spread, "tensor", 0, 0)
     weight_all = lax.all_gather(out_weight, "seq", axis=0, tiled=True)
-    projected = jnp.dot(
+    weight_all = weight_all.reshape(groups, channels, weight_all.shape[1])
+    projected = lax.dot_general(
         features,
         weight_all,
+        (((0, 2), (0, 1)), ((), ())),
         preferred_element_type=jnp.float32,
     )
     return projected.astype(jnp.bfloat16)

time: 293 us -> 214 us (0.73)
  the two profiles are of different devices: /device:TPU:1 before, /device:TPU:8 now
where the time goes in v2:
time: 214 us
  blocking collectives  101 us (47%)
  starting transfers between devices  43.8 us (20%)
  local copies, waits for them, and re-layouts  26.4 us (12%)
  matrix products  13.8 us (6%)
  between operations  13.7 us (6%)
  waiting for transfers between devices  8.54 us (4%)
  other arithmetic  6.23 us (3%)
    all_to_all x1, blocking collectives, finish(): features = lax.all_to_all(spread, 'tensor', 0, 0)  101 us
    ppermute x7, starting transfers between devices, passed_along(): return lax.ppermute(block, axis, route)  43.8 us
    unnamed x13, local copies, waits for them, and re-layouts  23.2 us
    ppermute x7, waiting for transfers between devices, passed_along(): return lax.ppermute(block, axis, route)  7.83 us
    dot_general x1, matrix products, finish(): lax.dot_general(features, weight_all, (((0, 2), (0, 1)), ((), ())), prefe...  7.69 us
    dot_general x1, matrix products, finish(): jnp.dot(lower, scaled, precision=PRECISE)  6.09 us
  transfers between devices with their start and end apart: 8, of which 4 were waited for; matrix products, arithmetic and copies ran while one was open for 17% of the time, Pallas kernels for 0%

profile of v2, /device:TPU:8, one launch (start us, length us, event | category | flops | bytes accessed | tf_op | source)
XLA Modules:
  0.0 213.8 jit_solution(15685891067531977818)
XLA Ops:
  6.5 0.7 all-gather.2.cloned.1.call-update
  7.3 0.8 slice.35
  8.0 1.7 collective-permute-start
  9.8 0.9 fusion.14
  10.7 0.8 copy.10
  11.4 1.4 maximum_convert_fusion
  13.4 1.1 mul.194
  14.5 8.0 %copy.11 = f32[32,8,16,512]{3,1,2,0:T(8,128)S(1)} copy(f32[32,8,16,512]{3,2,1,0:T(8,128)S(1)} %bitcast.37) | data formatting | bytes 16777216
  22.5 6.1 %fusion.2 = f32[256,8192]{1,0:T(8,128)S(1)} fusion(f32[256,8192]{1,0:T(8,128)S(1)} %bitcast.36, f32[8192]{0:T(1024)S(1)} %bitcast.39), kind=kOutput, calls=%fused_computation.3 | convolution fusion | flops 6446710784 | bytes 16809984 | tf_op jit(solution)/shard_map/dot_general | solution.py:59
  28.6 3.2 %copy-done = f32[256,8192]{1,0:T(8,128)} copy-done((f32[256,8192]{1,0:T(8,128)}, f32[256,8192]{1,0:T(8,128)S(1)}, u32[]{:S(2)}) %copy-start) | copy-done | bytes 8388632
  32.0 4.6 %collective-permute-start.1 = (f32[16,512]{1,0:T(8,128)S(1)}, f32[16,512]{1,0:T(8,128)S(1)}, u32[]{:S(2)}, u32[]{:S(2)}) collective-permute-start(f32[16,512]{1,0:T(8,128)S(1)} %exponential_multiply_fusion), channel_id=1, source_target_pairs={{0,16},{16,32},{32,48},{48,64},{64,80},{80,96},{96,112},{112,128},... | collective-permute-start | bytes 98312 | tf_op jit(solution)/shard_map/ppermute | solution.py:16
  36.5 4.3 %collective-permute-start.2 = (f32[16,512]{1,0:T(8,128)S(1)}, f32[16,512]{1,0:T(8,128)S(1)}, u32[]{:S(2)}, u32[]{:S(2)}) collective-permute-start(f32[16,512]{1,0:T(8,128)S(1)} %exponential_multiply_fusion), channel_id=1, source_target_pairs={{0,32},{16,48},{32,64},{48,80},{64,96},{80,112},{96,128},{112,144}... | collective-permute-start | bytes 98312 | tf_op jit(solution)/shard_map/ppermute | solution.py:16
  40.8 1.9 collective-permute-done.2
  42.8 4.8 %collective-permute-start.3 = (f32[16,512]{1,0:T(8,128)S(1)}, f32[16,512]{1,0:T(8,128)S(1)}, u32[]{:S(2)}, u32[]{:S(2)}) collective-permute-start(f32[16,512]{1,0:T(8,128)S(1)} %multiply_add_fusion.3), channel_id=1, source_target_pairs={{0,32},{16,48},{32,64},{48,80},{64,96},{80,112},{96,128},{112,144}... | collective-permute-start | bytes 98312 | tf_op jit(solution)/shard_map/ppermute | solution.py:16
  47.5 2.0 collective-permute-done.3
  49.6 7.7 %collective-permute-start.4 = (f32[16,512]{1,0:T(8,128)S(1)}, f32[16,512]{1,0:T(8,128)S(1)}, u32[]{:S(2)}, u32[]{:S(2)}) collective-permute-start(f32[16,512]{1,0:T(8,128)S(1)} %multiply_add_fusion.2), channel_id=1, source_target_pairs={{0,64},{16,80},{32,96},{48,112},{64,128},{80,144},{96,160},{112,17... | collective-permute-start | bytes 98312 | tf_op jit(solution)/shard_map/ppermute | solution.py:16
  57.2 1.9 collective-permute-done.4
  59.1 12.5 %collective-permute-start.5 = (f32[16,512]{1,0:T(8,128)S(1)}, f32[16,512]{1,0:T(8,128)S(1)}, u32[]{:S(2)}, u32[]{:S(2)}) collective-permute-start(f32[16,512]{1,0:T(8,128)S(1)} %multiply_add_fusion.1), channel_id=1, source_target_pairs={{0,128},{16,144},{32,160},{48,176},{64,192},{80,208},{96,224},{112... | collective-permute-start | bytes 98312 | tf_op jit(solution)/shard_map/ppermute | solution.py:16
  71.7 2.0 collective-permute-done.5
  73.7 8.2 %collective-permute-start.6 = (f32[16,512]{1,0:T(8,128)S(1)}, f32[16,512]{1,0:T(8,128)S(1)}, u32[]{:S(2)}, u32[]{:S(2)}) collective-permute-start(f32[16,512]{1,0:T(8,128)S(1)} %multiply_add_fusion), channel_id=1, source_target_pairs={{0,256},{16,272},{32,288},{48,304},{64,320},{80,336},{96,352},{112... | collective-permute-start | bytes 98312 | tf_op jit(solution)/shard_map/ppermute | solution.py:16
  82.0 11.1 %copy.12 = f32[32,8,16,512]{3,2,1,0:T(8,128)S(1)} copy(f32[32,8,16,512]{3,1,2,0:T(8,128)} %bitcast.35) | data formatting | bytes 16777216
  93.2 3.9 %fusion.1 = f32[256,512]{1,0:T(8,128)S(1)} fusion(f32[32,8,16,512]{3,2,1,0:T(8,128)S(1)} %copy.12, f32[16,512]{1,0:T(8,128)S(1)} %get-tuple-element.6, f32[16,512]{1,0:T(8,128)S(1)} %get-tuple-element.7, f32[16,512]{1,0:T(8,128)S(1)} %get-tuple-element.5), kind=kLoop, calls=%fused_computation.2 | loop fusion | flops 10354688 | bytes 9011200 | tf_op jit(solution)/shard_map/reduce_sum | solution.py:64
  97.8 101.5 %all_to_all.5 = bf16[16,256,512]{2,1,0:T(8,128)(2,1)} all-to-all(bf16[16,256,512]{2,1,0:T(8,128)(2,1)S(1)} %broadcast_in_dim.5), channel_id=1, replica_groups=mesh['seq'=32,'tensor'=16] {'tensor'}, dimensions={0} | all-to-all | bytes 8388608 | tf_op jit(solution)/shard_map/all_to_all | solution.py:69
  199.3 7.7 %fusion.10 = bf16[256,512]{1,0:T(8,128)(2,1)} fusion(bf16[16,256,512]{2,1,0:T(8,128)(2,1)} %all_to_all.5, bf16[16,512,512]{2,1,0:T(8,128)(2,1)} %bitcast.41), kind=kOutput, calls=%fused_computation.15 | convolution fusion | flops 2147614720 | bytes 12845056 | tf_op jit(solution)/shard_map/dot_general | solution.py:72
  (26 shorter events, 1.4 us)
Async XLA Ops:
  6.5 192.7 %all-gather.2.cloned.1.call-start = ((), (), s32[]{:S(2)}) async-start(), calls=%async_computation.1 | async-start | bytes 8650752 | tf_op jit(solution)/shard_map/all_gather | solution.py:70
  8.0 3.4 %collective-permute-start = (bf16[3,2,512]{2,1,0:T(2,128)(2,1)S(1)}, bf16[3,2,512]{2,1,0:T(2,128)(2,1)S(1)}, u32[]{:S(2)}, u32[]{:S(2)}) collective-permute-start(bf16[3,2,512]{2,1,0:T(2,128)(2,1)S(1)} %slice.35), channel_id=1, source_target_pairs={{0,16},{16,32},{32,48},{48,64},{64,80},{80,96},{96,112},{112,128},... | collective-permute-start | bytes 18440 | tf_op jit(solution)/shard_map/ppermute | solution.py:16
  22.5 9.5 %copy-start.1 = (f32[16,512]{1,0:T(8,128)S(1)}, f32[16,512]{1,0:T(8,128)}, u32[]{:S(2)}) copy-start(f32[16,512]{1,0:T(8,128)} %param.8) | copy-start | bytes 98308
  28.6 3.2 %copy-start = (f32[256,8192]{1,0:T(8,128)}, f32[256,8192]{1,0:T(8,128)S(1)}, u32[]{:S(2)}) copy-start(f32[256,8192]{1,0:T(8,128)S(1)} %fusion.2) | copy-start | bytes 25165828
  32.0 8.9 %collective-permute-start.1 = (f32[16,512]{1,0:T(8,128)S(1)}, f32[16,512]{1,0:T(8,128)S(1)}, u32[]{:S(2)}, u32[]{:S(2)}) collective-permute-start(f32[16,512]{1,0:T(8,128)S(1)} %exponential_multiply_fusion), channel_id=1, source_target_pairs={{0,16},{16,32},{32,48},{48,64},{64,80},{80,96},{96,112},{112,128},... | collective-permute-start | bytes 98312 | tf_op jit(solution)/shard_map/ppermute | solution.py:16
  36.5 6.2 %collective-permute-start.2 = (f32[16,512]{1,0:T(8,128)S(1)}, f32[16,512]{1,0:T(8,128)S(1)}, u32[]{:S(2)}, u32[]{:S(2)}) collective-permute-start(f32[16,512]{1,0:T(8,128)S(1)} %exponential_multiply_fusion), channel_id=1, source_target_pairs={{0,32},{16,48},{32,64},{48,80},{64,96},{80,112},{96,128},{112,144}... | collective-permute-start | bytes 98312 | tf_op jit(solution)/shard_map/ppermute | solution.py:16
  42.8 6.8 %collective-permute-start.3 = (f32[16,512]{1,0:T(8,128)S(1)}, f32[16,512]{1,0:T(8,128)S(1)}, u32[]{:S(2)}, u32[]{:S(2)}) collective-permute-start(f32[16,512]{1,0:T(8,128)S(1)} %multiply_add_fusion.3), channel_id=1, source_target_pairs={{0,32},{16,48},{32,64},{48,80},{64,96},{80,112},{96,128},{112,144}... | collective-permute-start | bytes 98312 | tf_op jit(solution)/shard_map/ppermute | solution.py:16
  49.6 9.5 %collective-permute-start.4 = (f32[16,512]{1,0:T(8,128)S(1)}, f32[16,512]{1,0:T(8,128)S(1)}, u32[]{:S(2)}, u32[]{:S(2)}) collective-permute-start(f32[16,512]{1,0:T(8,128)S(1)} %multiply_add_fusion.2), channel_id=1, source_target_pairs={{0,64},{16,80},{32,96},{48,112},{64,128},{80,144},{96,160},{112,17... | collective-permute-start | bytes 98312 | tf_op jit(solution)/shard_map/ppermute | solution.py:16
  59.1 14.6 %collective-permute-start.5 = (f32[16,512]{1,0:T(8,128)S(1)}, f32[16,512]{1,0:T(8,128)S(1)}, u32[]{:S(2)}, u32[]{:S(2)}) collective-permute-start(f32[16,512]{1,0:T(8,128)S(1)} %multiply_add_fusion.1), channel_id=1, source_target_pairs={{0,128},{16,144},{32,160},{48,176},{64,192},{80,208},{96,224},{112... | collective-permute-start | bytes 98312 | tf_op jit(solution)/shard_map/ppermute | solution.py:16
  73.7 19.4 %collective-permute-start.6 = (f32[16,512]{1,0:T(8,128)S(1)}, f32[16,512]{1,0:T(8,128)S(1)}, u32[]{:S(2)}, u32[]{:S(2)}) collective-permute-start(f32[16,512]{1,0:T(8,128)S(1)} %multiply_add_fusion), channel_id=1, source_target_pairs={{0,256},{16,272},{32,288},{48,304},{64,320},{80,336},{96,352},{112... | collective-permute-start | bytes 98312 | tf_op jit(solution)/shard_map/ppermute | solution.py:16
  81.9 11.2 %copy-start.2 = (f32[16,512]{1,0:T(8,128)S(1)}, f32[16,512]{1,0:T(8,128)}, u32[]{:S(2)}) copy-start(f32[16,512]{1,0:T(8,128)} %param.9) | copy-start | bytes 98308
  93.1 4.0 %copy-start.3 = (f32[512]{0:T(512)S(1)}, f32[512]{0:T(512)}, u32[]{:S(2)}) copy-start(f32[512]{0:T(512)} %param.10) | copy-start | bytes 6148
Sparse Core Ops, SparseCore 0:
  9.5 80.8 all-gather.1

commit v3 on v1

--- a/solution.py
+++ b/solution.py
@@ -14,6 +14,34 @@
     devices = range(lax.axis_size(axis))
     route = [(i - distance, i) for i in devices if i - distance in devices]
     return lax.ppermute(block, axis, route)
+
+
+def shifted(block, axis, route):
+    return lax.ppermute(block, axis, route)
+
+
+def ring_gather(block, axis, ring):
+    size = lax.axis_size(axis)
+    ring = min(ring, size)
+    halves = size // ring
+    place = lax.axis_index(axis)
+    if halves == 2:
+        partner = shifted(block, axis, [(i, i ^ ring) for i in range(size)])
+        first = place // ring == 0
+        chunk = jnp.where(first, jnp.stack([block, partner]), jnp.stack([partner, block]))
+    else:
+        chunk = block[None]
+    forward = [(i, (i // ring) * ring + (i % ring + 1) % ring) for i in range(size)]
+    backward = [(i, (i // ring) * ring + (i % ring - 1) % ring) for i in range(size)]
+    ahead, behind = [], []
+    up, down = chunk, chunk
+    for step in range(ring // 2):
+        up = shifted(up, axis, forward)
+        behind.append(up)
+        if step < (ring - 1) // 2:
+            down = shifted(down, axis, backward)
+            ahead.append(down)
+    return jnp.stack([chunk] + ahead + behind[::-1])
 
 
 def entering_state(local_state, rate, tokens_here, axis):
@@ -64,12 +92,15 @@
     long_part = jnp.sum(mode_weight[None] * shrink * total, axis=1)
     long_part = long_part + skip_gain[None, :] * product
     mixed_local = (filtered[0] * long_part).astype(jnp.bfloat16)
-    features = lax.all_gather(mixed_local, "tensor", axis=1, tiled=True)
+    features = ring_gather(mixed_local, "tensor", 8)
     weight_all = lax.all_gather(out_weight, "seq", axis=0, tiled=True)
-    projected = jnp.dot(
-        features,
-        weight_all,
-        preferred_element_type=jnp.float32,
+    ring = features.shape[0]
+    halves = features.shape[1]
+    weight_all = weight_all.reshape(halves, ring, channels, weight_all.shape[1])
+    place = lax.axis_index("tensor") % ring
+    weight_all = jnp.roll(weight_all, -place, axis=1)
+    projected = jnp.einsum(
+        "rhtc,hrco->to", features, weight_all, preferred_element_type=jnp.float32
     )
     return projected.astype(jnp.bfloat16)
 

time: 293 us -> 183 us (0.62)
  the two profiles are of different devices: /device:TPU:1 before, /device:TPU:4 now
where the time goes in v3:
time: 183 us; the launch traced here: 182 us
  starting transfers between devices  70.4 us (38%)
  waiting for transfers between devices  42.9 us (23%)
  local copies, waits for them, and re-layouts  31.8 us (17%)
  matrix products  15.7 us (9%)
  between operations  13.8 us (8%)
  other arithmetic  7.45 us (4%)
    ppermute x7, starting transfers between devices, passed_along(): return lax.ppermute(block, axis, route)  43.3 us
    ppermute x8, waiting for transfers between devices, shifted(): return lax.ppermute(block, axis, route)  33.8 us
    unnamed x19, local copies, waits for them, and re-layouts  28.1 us
    ppermute x8, starting transfers between devices, shifted(): return lax.ppermute(block, axis, route)  27.1 us
    dot_general x1, matrix products, finish(): jnp.einsum('rhtc,hrco->to', features, weight_all, preferred_element_type=...  9.64 us
    ppermute x7, waiting for transfers between devices, passed_along(): return lax.ppermute(block, axis, route)  8.41 us
    dot_general x1, matrix products, finish(): jnp.dot(lower, scaled, precision=PRECISE)  6.09 us
    reduce_sum x1, other arithmetic, finish(): long_part = jnp.sum(mode_weight[None] * shrink * total, axis=1)  3.95 us
  transfers between devices with their start and end apart: 16, of which 10 were waited for; matrix products, arithmetic and copies ran while one was open for 23% of the time, Pallas kernels for 0%

profile of v3, /device:TPU:4, one launch (start us, length us, event | category | flops | bytes accessed | tf_op | source)
XLA Modules:
  0.0 182.1 jit_solution(16032212009889153837)
XLA Ops:
  14.5 8.0 %copy.26 = f32[32,8,16,512]{3,1,2,0:T(8,128)S(1)} copy(f32[32,8,16,512]{3,2,1,0:T(8,128)S(1)} %bitcast.75) | data formatting | bytes 16777216
  22.5 6.1 %fusion.3 = f32[256,8192]{1,0:T(8,128)S(1)} fusion(f32[256,8192]{1,0:T(8,128)S(1)} %bitcast.74, f32[8192]{0:T(1024)S(1)} %bitcast.80), kind=kOutput, calls=%fused_computation.6 | convolution fusion | flops 6446710784 | bytes 16809984 | tf_op jit(solution)/shard_map/dot_general | solution.py:87
  28.6 3.2 %copy-done = f32[256,8192]{1,0:T(8,128)} copy-done((f32[256,8192]{1,0:T(8,128)}, f32[256,8192]{1,0:T(8,128)S(1)}, u32[]{:S(2)}) %copy-start) | copy-done | bytes 8388632
  32.0 4.6 %collective-permute-start.1 = (f32[16,512]{1,0:T(8,128)S(1)}, f32[16,512]{1,0:T(8,128)S(1)}, u32[]{:S(2)}, u32[]{:S(2)}) collective-permute-start(f32[16,512]{1,0:T(8,128)S(1)} %exponential_multiply_fusion), channel_id=1, source_target_pairs={{0,16},{16,32},{32,48},{48,64},{64,80},{80,96},{96,112},{112,128},... | collective-permute-start | bytes 98312 | tf_op jit(solution)/shard_map/ppermute | solution.py:16
  36.6 4.3 %collective-permute-start.2 = (f32[16,512]{1,0:T(8,128)S(1)}, f32[16,512]{1,0:T(8,128)S(1)}, u32[]{:S(2)}, u32[]{:S(2)}) collective-permute-start(f32[16,512]{1,0:T(8,128)S(1)} %exponential_multiply_fusion), channel_id=1, source_target_pairs={{0,32},{16,48},{32,64},{48,80},{64,96},{80,112},{96,128},{112,144}... | collective-permute-start | bytes 98312 | tf_op jit(solution)/shard_map/ppermute | solution.py:16
  42.9 4.6 %collective-permute-start.3 = (f32[16,512]{1,0:T(8,128)S(1)}, f32[16,512]{1,0:T(8,128)S(1)}, u32[]{:S(2)}, u32[]{:S(2)}) collective-permute-start(f32[16,512]{1,0:T(8,128)S(1)} %multiply_add_fusion.3), channel_id=1, source_target_pairs={{0,32},{16,48},{32,64},{48,80},{64,96},{80,112},{96,128},{112,144}... | collective-permute-start | bytes 98312 | tf_op jit(solution)/shard_map/ppermute | solution.py:16
  49.6 7.6 %collective-permute-start.4 = (f32[16,512]{1,0:T(8,128)S(1)}, f32[16,512]{1,0:T(8,128)S(1)}, u32[]{:S(2)}, u32[]{:S(2)}) collective-permute-start(f32[16,512]{1,0:T(8,128)S(1)} %multiply_add_fusion.2), channel_id=1, source_target_pairs={{0,64},{16,80},{32,96},{48,112},{64,128},{80,144},{96,160},{112,17... | collective-permute-start | bytes 98312 | tf_op jit(solution)/shard_map/ppermute | solution.py:16
  59.3 12.4 %collective-permute-start.5 = (f32[16,512]{1,0:T(8,128)S(1)}, f32[16,512]{1,0:T(8,128)S(1)}, u32[]{:S(2)}, u32[]{:S(2)}) collective-permute-start(f32[16,512]{1,0:T(8,128)S(1)} %multiply_add_fusion.1), channel_id=1, source_target_pairs={{0,128},{16,144},{32,160},{48,176},{64,192},{80,208},{96,224},{112... | collective-permute-start | bytes 98312 | tf_op jit(solution)/shard_map/ppermute | solution.py:16
  73.9 8.2 %collective-permute-start.6 = (f32[16,512]{1,0:T(8,128)S(1)}, f32[16,512]{1,0:T(8,128)S(1)}, u32[]{:S(2)}, u32[]{:S(2)}) collective-permute-start(f32[16,512]{1,0:T(8,128)S(1)} %multiply_add_fusion), channel_id=1, source_target_pairs={{0,256},{16,272},{32,288},{48,304},{64,320},{80,336},{96,352},{112... | collective-permute-start | bytes 98312 | tf_op jit(solution)/shard_map/ppermute | solution.py:16
  82.1 11.1 %copy.27 = f32[32,8,16,512]{3,2,1,0:T(8,128)S(1)} copy(f32[32,8,16,512]{3,1,2,0:T(8,128)} %bitcast.73) | data formatting | bytes 16777216
  93.2 3.9 %fusion.2 = f32[256,512]{1,0:T(8,128)S(1)} fusion(f32[32,8,16,512]{3,2,1,0:T(8,128)S(1)} %copy.27, f32[16,512]{1,0:T(8,128)S(1)} %get-tuple-element.6, f32[16,512]{1,0:T(8,128)S(1)} %get-tuple-element.7, f32[16,512]{1,0:T(8,128)S(1)} %get-tuple-element.5), kind=kLoop, calls=%fused_computation.5 | loop fusion | flops 10354688 | bytes 9011200 | tf_op jit(solution)/shard_map/reduce_sum | solution.py:92
  100.3 6.9 %collective-permute-done.7 = bf16[256,512]{1,0:T(8,128)(2,1)S(1)} collective-permute-done((bf16[256,512]{1,0:T(8,128)(2,1)S(1)}, bf16[256,512]{1,0:T(8,128)(2,1)S(1)}, u32[]{:S(2)}, u32[]{:S(2)}) %collective-permute-start.7) | collective-permute-done | bytes 262176 | tf_op jit(solution)/shard_map/ppermute | solution.py:20
  107.3 3.7 %collective-permute-start.11 = (bf16[2,256,512]{2,1,0:T(8,128)(2,1)S(1)}, bf16[2,256,512]{2,1,0:T(8,128)(2,1)S(1)}, u32[]{:S(2)}, u32[]{:S(2)}) collective-permute-start(bf16[2,256,512]{2,1,0:T(8,128)(2,1)S(1)} %maximum_select_fusion.1), channel_id=1, source_target_pairs={{0,1},{1,2},{2,3},{3,4},{4,5},{5,6},{6,7},{7,0},{8,9},{9,10},{10,1... | collective-permute-start | bytes 1572872 | tf_op jit(solution)/shard_map/ppermute | solution.py:20
  111.0 3.5 %collective-permute-start.8 = (bf16[2,256,512]{2,1,0:T(8,128)(2,1)S(1)}, bf16[2,256,512]{2,1,0:T(8,128)(2,1)S(1)}, u32[]{:S(2)}, u32[]{:S(2)}) collective-permute-start(bf16[2,256,512]{2,1,0:T(8,128)(2,1)S(1)} %maximum_select_fusion.1), channel_id=1, source_target_pairs={{0,7},{1,0},{2,1},{3,2},{4,3},{5,4},{6,5},{7,6},{8,15},{9,8},{10,9... | collective-permute-start | bytes 1572872 | tf_op jit(solution)/shard_map/ppermute | solution.py:20
  114.5 5.7 %collective-permute-done.11 = bf16[2,256,512]{2,1,0:T(8,128)(2,1)S(1)} collective-permute-done((bf16[2,256,512]{2,1,0:T(8,128)(2,1)S(1)}, bf16[2,256,512]{2,1,0:T(8,128)(2,1)S(1)}, u32[]{:S(2)}, u32[]{:S(2)}) %collective-permute-start.11) | collective-permute-done | bytes 524320 | tf_op jit(solution)/shard_map/ppermute | solution.py:20
  120.2 3.7 %collective-permute-start.12 = (bf16[2,256,512]{2,1,0:T(8,128)(2,1)S(1)}, bf16[2,256,512]{2,1,0:T(8,128)(2,1)S(1)}, u32[]{:S(2)}, u32[]{:S(2)}) collective-permute-start(bf16[2,256,512]{2,1,0:T(8,128)(2,1)S(1)} %collective-permute-done.11), channel_id=1, source_target_pairs={{0,1},{1,2},{2,3},{3,4},{4,5},{5,6},{6,7},{7,0},{8,9},{9,10},{10,1... | collective-permute-start | bytes 1572872 | tf_op jit(solution)/shard_map/ppermute | solution.py:20
  124.0 3.5 %collective-permute-start.9 = (bf16[2,256,512]{2,1,0:T(8,128)(2,1)S(1)}, bf16[2,256,512]{2,1,0:T(8,128)(2,1)S(1)}, u32[]{:S(2)}, u32[]{:S(2)}) collective-permute-start(bf16[2,256,512]{2,1,0:T(8,128)(2,1)S(1)} %collective-permute-done.8), channel_id=1, source_target_pairs={{0,7},{1,0},{2,1},{3,2},{4,3},{5,4},{6,5},{7,6},{8,15},{9,8},{10,9... | collective-permute-start | bytes 1572872 | tf_op jit(solution)/shard_map/ppermute | solution.py:20
  127.6 7.1 %collective-permute-done.12 = bf16[2,256,512]{2,1,0:T(8,128)(2,1)S(1)} collective-permute-done((bf16[2,256,512]{2,1,0:T(8,128)(2,1)S(1)}, bf16[2,256,512]{2,1,0:T(8,128)(2,1)S(1)}, u32[]{:S(2)}, u32[]{:S(2)}) %collective-permute-start.12) | collective-permute-done | bytes 524320 | tf_op jit(solution)/shard_map/ppermute | solution.py:20
  134.7 3.3 %collective-permute-start.13 = (bf16[2,256,512]{2,1,0:T(8,128)(2,1)S(1)}, bf16[2,256,512]{2,1,0:T(8,128)(2,1)S(1)}, u32[]{:S(2)}, u32[]{:S(2)}) collective-permute-start(bf16[2,256,512]{2,1,0:T(8,128)(2,1)S(1)} %collective-permute-done.12), channel_id=1, source_target_pairs={{0,1},{1,2},{2,3},{3,4},{4,5},{5,6},{6,7},{7,0},{8,9},{9,10},{10,1... | collective-permute-start | bytes 1572872 | tf_op jit(solution)/shard_map/ppermute | solution.py:20
  138.0 3.8 %collective-permute-start.10 = (bf16[2,256,512]{2,1,0:T(8,128)(2,1)S(1)}, bf16[2,256,512]{2,1,0:T(8,128)(2,1)S(1)}, u32[]{:S(2)}, u32[]{:S(2)}) collective-permute-start(bf16[2,256,512]{2,1,0:T(8,128)(2,1)S(1)} %collective-permute-done.9), channel_id=1, source_target_pairs={{0,7},{1,0},{2,1},{3,2},{4,3},{5,4},{6,5},{7,6},{8,15},{9,8},{10,9... | collective-permute-start | bytes 1572872 | tf_op jit(solution)/shard_map/ppermute | solution.py:20
  142.7 7.3 %collective-permute-done.13 = bf16[2,256,512]{2,1,0:T(8,128)(2,1)S(1)} collective-permute-done((bf16[2,256,512]{2,1,0:T(8,128)(2,1)S(1)}, bf16[2,256,512]{2,1,0:T(8,128)(2,1)S(1)}, u32[]{:S(2)}, u32[]{:S(2)}) %collective-permute-start.13) | collective-permute-done | bytes 524320 | tf_op jit(solution)/shard_map/ppermute | solution.py:20
  150.0 3.1 %collective-permute-start.14 = (bf16[2,256,512]{2,1,0:T(8,128)(2,1)S(1)}, bf16[2,256,512]{2,1,0:T(8,128)(2,1)S(1)}, u32[]{:S(2)}, u32[]{:S(2)}) collective-permute-start(bf16[2,256,512]{2,1,0:T(8,128)(2,1)S(1)} %collective-permute-done.13), channel_id=1, source_target_pairs={{0,1},{1,2},{2,3},{3,4},{4,5},{5,6},{6,7},{7,0},{8,9},{9,10},{10,1... | collective-permute-start | bytes 1572872 | tf_op jit(solution)/shard_map/ppermute | solution.py:20
  155.6 6.6 %collective-permute-done.14 = bf16[2,256,512]{2,1,0:T(8,128)(2,1)S(1)} collective-permute-done((bf16[2,256,512]{2,1,0:T(8,128)(2,1)S(1)}, bf16[2,256,512]{2,1,0:T(8,128)(2,1)S(1)}, u32[]{:S(2)}, u32[]{:S(2)}) %collective-permute-start.14) | collective-permute-done | bytes 524320 | tf_op jit(solution)/shard_map/ppermute | solution.py:20
  165.6 9.6 %fusion.16 = bf16[256,512]{1,0:T(8,128)(2,1)} fusion(bf16[8,2,256,512]{3,2,0,1:T(8,128)(2,1)} %bitcast_dynamic-update-slice_fusion.6, s32[]{:T(128)S(6)} %select_n.49, bf16[2,8,512,512]{3,2,1,0:T(8,128)(2,1)} %bitcast.82), kind=kOutput, calls=%fused_computation.19 | convolution fusion | flops 2151809024 | bytes 12845060 | tf_op jit(solution)/shard_map/rhtc,hrco->to/dot_general | solution.py:102
  (50 shorter events, 26.5 us)
Async XLA Ops:
  6.5 159.0 %all-gather.2.cloned.1.call-start = ((), (), s32[]{:S(2)}) async-start(), calls=%async_computation | async-start | bytes 8650752 | tf_op jit(solution)/shard_map/all_gather | solution.py:96
  8.0 3.4 %collective-permute-start = (bf16[3,2,512]{2,1,0:T(2,128)(2,1)S(1)}, bf16[3,2,512]{2,1,0:T(2,128)(2,1)S(1)}, u32[]{:S(2)}, u32[]{:S(2)}) collective-permute-start(bf16[3,2,512]{2,1,0:T(2,128)(2,1)S(1)} %slice.35), channel_id=1, source_target_pairs={{0,16},{16,32},{32,48},{48,64},{64,80},{80,96},{96,112},{112,128},... | collective-permute-start | bytes 18440 | tf_op jit(solution)/shard_map/ppermute | solution.py:16
  22.5 9.5 %copy-start.1 = (f32[16,512]{1,0:T(8,128)S(1)}, f32[16,512]{1,0:T(8,128)}, u32[]{:S(2)}) copy-start(f32[16,512]{1,0:T(8,128)} %param.8) | copy-start | bytes 98308
  28.6 3.2 %copy-start = (f32[256,8192]{1,0:T(8,128)}, f32[256,8192]{1,0:T(8,128)S(1)}, u32[]{:S(2)}) copy-start(f32[256,8192]{1,0:T(8,128)S(1)} %fusion.3) | copy-start | bytes 25165828
  32.0 8.9 %collective-permute-start.1 = (f32[16,512]{1,0:T(8,128)S(1)}, f32[16,512]{1,0:T(8,128)S(1)}, u32[]{:S(2)}, u32[]{:S(2)}) collective-permute-start(f32[16,512]{1,0:T(8,128)S(1)} %exponential_multiply_fusion), channel_id=1, source_target_pairs={{0,16},{16,32},{32,48},{48,64},{64,80},{80,96},{96,112},{112,128},... | collective-permute-start | bytes 98312 | tf_op jit(solution)/shard_map/ppermute | solution.py:16
  36.6 6.4 %collective-permute-start.2 = (f32[16,512]{1,0:T(8,128)S(1)}, f32[16,512]{1,0:T(8,128)S(1)}, u32[]{:S(2)}, u32[]{:S(2)}) collective-permute-start(f32[16,512]{1,0:T(8,128)S(1)} %exponential_multiply_fusion), channel_id=1, source_target_pairs={{0,32},{16,48},{32,64},{48,80},{64,96},{80,112},{96,128},{112,144}... | collective-permute-start | bytes 98312 | tf_op jit(solution)/shard_map/ppermute | solution.py:16
  42.9 6.7 %collective-permute-start.3 = (f32[16,512]{1,0:T(8,128)S(1)}, f32[16,512]{1,0:T(8,128)S(1)}, u32[]{:S(2)}, u32[]{:S(2)}) collective-permute-start(f32[16,512]{1,0:T(8,128)S(1)} %multiply_add_fusion.3), channel_id=1, source_target_pairs={{0,32},{16,48},{32,64},{48,80},{64,96},{80,112},{96,128},{112,144}... | collective-permute-start | bytes 98312 | tf_op jit(solution)/shard_map/ppermute | solution.py:16
  49.6 9.6 %collective-permute-start.4 = (f32[16,512]{1,0:T(8,128)S(1)}, f32[16,512]{1,0:T(8,128)S(1)}, u32[]{:S(2)}, u32[]{:S(2)}) collective-permute-start(f32[16,512]{1,0:T(8,128)S(1)} %multiply_add_fusion.2), channel_id=1, source_target_pairs={{0,64},{16,80},{32,96},{48,112},{64,128},{80,144},{96,160},{112,17... | collective-permute-start | bytes 98312 | tf_op jit(solution)/shard_map/ppermute | solution.py:16
  59.3 14.6 %collective-permute-start.5 = (f32[16,512]{1,0:T(8,128)S(1)}, f32[16,512]{1,0:T(8,128)S(1)}, u32[]{:S(2)}, u32[]{:S(2)}) collective-permute-start(f32[16,512]{1,0:T(8,128)S(1)} %multiply_add_fusion.1), channel_id=1, source_target_pairs={{0,128},{16,144},{32,160},{48,176},{64,192},{80,208},{96,224},{112... | collective-permute-start | bytes 98312 | tf_op jit(solution)/shard_map/ppermute | solution.py:16
  73.9 19.2 %collective-permute-start.6 = (f32[16,512]{1,0:T(8,128)S(1)}, f32[16,512]{1,0:T(8,128)S(1)}, u32[]{:S(2)}, u32[]{:S(2)}) collective-permute-start(f32[16,512]{1,0:T(8,128)S(1)} %multiply_add_fusion), channel_id=1, source_target_pairs={{0,256},{16,272},{32,288},{48,304},{64,320},{80,336},{96,352},{112... | collective-permute-start | bytes 98312 | tf_op jit(solution)/shard_map/ppermute | solution.py:16
  82.1 11.1 %copy-start.2 = (f32[16,512]{1,0:T(8,128)S(1)}, f32[16,512]{1,0:T(8,128)}, u32[]{:S(2)}) copy-start(f32[16,512]{1,0:T(8,128)} %param.9) | copy-start | bytes 98308
  93.2 4.0 %copy-start.3 = (f32[512]{0:T(512)S(1)}, f32[512]{0:T(512)}, u32[]{:S(2)}) copy-start(f32[512]{0:T(512)} %param.10) | copy-start | bytes 6148
  97.4 9.8 %collective-permute-start.7 = (bf16[256,512]{1,0:T(8,128)(2,1)S(1)}, bf16[256,512]{1,0:T(8,128)(2,1)S(1)}, u32[]{:S(2)}, u32[]{:S(2)}) collective-permute-start(bf16[256,512]{1,0:T(8,128)(2,1)S(1)} %fusion.21), channel_id=1, source_target_pairs={{0,8},{1,9},{2,10},{3,11},{4,12},{5,13},{6,14},{7,15},{8,0},{9,1},... | collective-permute-start | bytes 786440 | tf_op jit(solution)/shard_map/ppermute | solution.py:20
  107.3 12.9 %collective-permute-start.11 = (bf16[2,256,512]{2,1,0:T(8,128)(2,1)S(1)}, bf16[2,256,512]{2,1,0:T(8,128)(2,1)S(1)}, u32[]{:S(2)}, u32[]{:S(2)}) collective-permute-start(bf16[2,256,512]{2,1,0:T(8,128)(2,1)S(1)} %maximum_select_fusion.1), channel_id=1, source_target_pairs={{0,1},{1,2},{2,3},{3,4},{4,5},{5,6},{6,7},{7,0},{8,9},{9,10},{10,1... | collective-permute-start | bytes 1572872 | tf_op jit(solution)/shard_map/ppermute | solution.py:20
  111.0 13.0 %collective-permute-start.8 = (bf16[2,256,512]{2,1,0:T(8,128)(2,1)S(1)}, bf16[2,256,512]{2,1,0:T(8,128)(2,1)S(1)}, u32[]{:S(2)}, u32[]{:S(2)}) collective-permute-start(bf16[2,256,512]{2,1,0:T(8,128)(2,1)S(1)} %maximum_select_fusion.1), channel_id=1, source_target_pairs={{0,7},{1,0},{2,1},{3,2},{4,3},{5,4},{6,5},{7,6},{8,15},{9,8},{10,9... | collective-permute-start | bytes 1572872 | tf_op jit(solution)/shard_map/ppermute | solution.py:20
  120.2 14.4 %collective-permute-start.12 = (bf16[2,256,512]{2,1,0:T(8,128)(2,1)S(1)}, bf16[2,256,512]{2,1,0:T(8,128)(2,1)S(1)}, u32[]{:S(2)}, u32[]{:S(2)}) collective-permute-start(bf16[2,256,512]{2,1,0:T(8,128)(2,1)S(1)} %collective-permute-done.11), channel_id=1, source_target_pairs={{0,1},{1,2},{2,3},{3,4},{4,5},{5,6},{6,7},{7,0},{8,9},{9,10},{10,1... | collective-permute-start | bytes 1572872 | tf_op jit(solution)/shard_map/ppermute | solution.py:20
  124.0 13.9 %collective-permute-start.9 = (bf16[2,256,512]{2,1,0:T(8,128)(2,1)S(1)}, bf16[2,256,512]{2,1,0:T(8,128)(2,1)S(1)}, u32[]{:S(2)}, u32[]{:S(2)}) collective-permute-start(bf16[2,256,512]{2,1,0:T(8,128)(2,1)S(1)} %collective-permute-done.8), channel_id=1, source_target_pairs={{0,7},{1,0},{2,1},{3,2},{4,3},{5,4},{6,5},{7,6},{8,15},{9,8},{10,9... | collective-permute-start | bytes 1572872 | tf_op jit(solution)/shard_map/ppermute | solution.py:20
  134.7 15.3 %collective-permute-start.13 = (bf16[2,256,512]{2,1,0:T(8,128)(2,1)S(1)}, bf16[2,256,512]{2,1,0:T(8,128)(2,1)S(1)}, u32[]{:S(2)}, u32[]{:S(2)}) collective-permute-start(bf16[2,256,512]{2,1,0:T(8,128)(2,1)S(1)} %collective-permute-done.12), channel_id=1, source_target_pairs={{0,1},{1,2},{2,3},{3,4},{4,5},{5,6},{6,7},{7,0},{8,9},{9,10},{10,1... | collective-permute-start | bytes 1572872 | tf_op jit(solution)/shard_map/ppermute | solution.py:20
  138.0 16.8 %collective-permute-start.10 = (bf16[2,256,512]{2,1,0:T(8,128)(2,1)S(1)}, bf16[2,256,512]{2,1,0:T(8,128)(2,1)S(1)}, u32[]{:S(2)}, u32[]{:S(2)}) collective-permute-start(bf16[2,256,512]{2,1,0:T(8,128)(2,1)S(1)} %collective-permute-done.9), channel_id=1, source_target_pairs={{0,7},{1,0},{2,1},{3,2},{4,3},{5,4},{6,5},{7,6},{8,15},{9,8},{10,9... | collective-permute-start | bytes 1572872 | tf_op jit(solution)/shard_map/ppermute | solution.py:20
  150.0 12.3 %collective-permute-start.14 = (bf16[2,256,512]{2,1,0:T(8,128)(2,1)S(1)}, bf16[2,256,512]{2,1,0:T(8,128)(2,1)S(1)}, u32[]{:S(2)}, u32[]{:S(2)}) collective-permute-start(bf16[2,256,512]{2,1,0:T(8,128)(2,1)S(1)} %collective-permute-done.13), channel_id=1, source_target_pairs={{0,1},{1,2},{2,3},{3,4},{4,5},{5,6},{6,7},{7,0},{8,9},{9,10},{10,1... | collective-permute-start | bytes 1572872 | tf_op jit(solution)/shard_map/ppermute | solution.py:20
Sparse Core Ops, SparseCore 0:
  9.5 80.8 all-gather.1
